TPU v7x, 512 devices: a whole 4x4x16 slice. The times are simulated.
512 devices in a mesh: dp: 4 (over x), tensor: 128 (over y, z, core).
Axes of the slice: x: 4, y: 4, z: 16, core: 2. Of those that a mesh axis runs over, the one named last changes fastest.
Arguments:
- stream: bfloat16 [32768, 2560], P(('dp', 'tensor')), parts along dimension 0, may hold values from -6 to 6
- queries: bfloat16 [512, 2560], P(('dp', 'tensor')), parts along dimension 0, may hold values from -170 to 170
- fresh_entries: bfloat16 [512, 1024], P(('dp', 'tensor')), parts along dimension 0, may hold values from -6 to 6
- paged_store_cache: bfloat16 [2560, 2, 128, 512], P(('dp', 'tensor')), parts along dimension 0, may hold values from -6 to 6
- page_table: int32 [512, 32], P('dp'), parts along dimension 0, may hold values from -1 to 639, as said below
- cache_length: int32 [512], P('dp'), parts along dimension 0, may hold values from 1 to 4096, as said below
- out_proj: bfloat16 [2560, 2560], P(None, 'tensor'), may hold values from -0.125 to 0.125
- norm_gain: bfloat16 [2560], replicated, may hold values from 0.099609375 to 1.8984375
- router: bfloat16 [2560, 64], replicated, may hold values from -0.125 to 0.125
- routes: int32 [32768, 6], P(('dp', 'tensor')), parts along dimension 0, may hold values from 0 to 63, as said below
- gate_up: bfloat16 [2, 24576, 2560], P(None, 'tensor'), may hold values from -0.125 to 0.125
- down_proj: bfloat16 [24576, 2560], P('tensor'), may hold values from -0.15625 to 0.15625
Outputs:
- layer_out: bfloat16 [32768, 2560], P(('dp', 'tensor')), parts along dimension 0
There are 4 independent parts, one for each index of `dp`. A program takes and returns all parts, laid end to end along the dimension named above; an argument that names none is the same for every part. Nothing has to cross between parts.
Inputs may be any that keep to these rules, and one draw needn't show every extreme that they name: `routes`: each row names 6 different experts. The rows of one device name each expert at most 6 times, and on every device one and the same expert below 16 is named exactly 6 times. `page_table`: row r lists in order the pages of request r's cache, ceil(cache_length[r] / 128) of them, then -1; every page belongs to exactly one request. `cache_length`: some request's cache holds exactly 4096 tokens.
All inputs are finite; a program needn't handle non-finite values.
Results may differ from a plain program's by a relative error of at most 0.0045.
Values may be sent and summed in bfloat16 or wider, within the bound.
No kernel may reach another device: no remote copies, remote signals or barrier semaphores. Data moves between devices by JAX's collectives and lax.ppermute only.
A program may use at most 64 MiB of HBM per device.

v0:
```python
import math
import jax
import jax.numpy as jnp
from jax import lax
from jax.sharding import PartitionSpec as P

QUERY_HEADS = 20
KEY_VALUE_HEADS = 4
HEAD_SIZE = 128
GROUP = 8
CAP = 6
NEG_FILL = -1e30
EPSILON = 1e-05


def finish_context(maxima, totals, accum, local_queries, local_entries):
    entry_count = local_queries.shape[0]
    key_value_width = KEY_VALUE_HEADS * HEAD_SIZE
    query_vector = local_queries.reshape(
        entry_count, KEY_VALUE_HEADS, QUERY_HEADS // KEY_VALUE_HEADS, HEAD_SIZE
    )
    token_key = local_entries[:, :key_value_width].reshape(entry_count, KEY_VALUE_HEADS, HEAD_SIZE)
    token_value = (
        local_entries[:, key_value_width:]
        .reshape(entry_count, KEY_VALUE_HEADS, HEAD_SIZE)
        .astype(jnp.float32)
    )
    own_score = jnp.einsum(
        "rhgd,rhd->rhg", query_vector, token_key, preferred_element_type=jnp.float32
    ) * (1.0 / math.sqrt(HEAD_SIZE))
    joined = jnp.maximum(maxima, own_score)
    old_coef = jnp.exp(maxima - joined)
    own_weight = jnp.exp(own_score - joined)
    totals = totals * old_coef + own_weight
    accum = accum * old_coef[..., None] + own_weight[..., None] * token_value[:, :, None, :]
    return (
        (accum / totals[..., None])
        .reshape(entry_count, QUERY_HEADS * HEAD_SIZE)
        .astype(jnp.bfloat16)
    )


def local_parts(query_all, paged_store_cache, page_table, cache_length, my_index):
    request_page_count = paged_store_cache.shape[0]
    page_length = paged_store_cache.shape[2]
    longest = page_table.shape[1]
    query_groups = QUERY_HEADS // KEY_VALUE_HEADS
    global_ids = my_index * request_page_count + jnp.arange(request_page_count, dtype=jnp.int32)
    matched = page_table[None, :, :] == global_ids[:, None, None]
    owner = jnp.any(matched, axis=2)
    position = jnp.sum(
        jnp.where(matched, jnp.arange(longest, dtype=jnp.int32)[None, None, :], 0), axis=(1, 2)
    )
    length_here = jnp.sum(jnp.where(owner, cache_length[None, :], 0), axis=1)
    query_page_scores = jnp.dot(
        owner.astype(jnp.bfloat16), query_all, preferred_element_type=jnp.float32
    ).astype(jnp.bfloat16)
    query_page_scores = query_page_scores.reshape(
        request_page_count, KEY_VALUE_HEADS, query_groups, HEAD_SIZE
    )
    key_matrix = paged_store_cache[:, 0].reshape(
        request_page_count, page_length, KEY_VALUE_HEADS, HEAD_SIZE
    )
    value_matrix = (
        paged_store_cache[:, 1]
        .reshape(request_page_count, page_length, KEY_VALUE_HEADS, HEAD_SIZE)
        .astype(jnp.float32)
    )
    scores = jnp.einsum(
        "phgd,pthd->phgt", query_page_scores, key_matrix, preferred_element_type=jnp.float32
    ) * (1.0 / math.sqrt(HEAD_SIZE))
    offsets = jnp.arange(page_length, dtype=jnp.int32)
    valid = position[:, None] * page_length + offsets[None, :] < length_here[:, None]
    scores = jnp.where(valid[:, None, None, :], scores, NEG_FILL)
    page_max = jnp.max(scores, axis=-1)
    weights = jnp.exp(scores - page_max[..., None])
    page_total = jnp.sum(weights, axis=-1)
    page_accum = jnp.einsum("phgt,pthd->phgd", weights, value_matrix)
    owned = owner[:, :, None, None]
    request_max = jnp.max(jnp.where(owned, page_max[:, None], NEG_FILL), axis=0)
    coef = jnp.where(owned, jnp.exp(page_max[:, None] - request_max[None]), 0.0)
    request_total = jnp.sum(coef * page_total[:, None], axis=0)
    request_accum = jnp.einsum("prhg,phgd->rhgd", coef, page_accum)
    return (request_max, request_total, request_accum)


def local(
    stream,
    queries,
    fresh_entries,
    paged_store_cache,
    page_table,
    cache_length,
    out_proj,
    norm_gain,
    router,
    routes,
    gate_up,
    down_proj,
):
    tensor_count = lax.axis_size("tensor")
    my_index = lax.axis_index("tensor")
    dec_rows = queries.shape[0]
    query_all, entries_all = (
        lax.all_gather(queries, "tensor", axis=0, tiled=True),
        lax.all_gather(fresh_entries, "tensor", axis=0, tiled=True),
    )
    request_max, request_total, request_accum = local_parts(
        query_all, paged_store_cache, page_table, cache_length, my_index
    )
    maxima = lax.pmax(request_max, "tensor")
    rescale = jnp.exp(request_max - maxima)
    totals, accum = lax.psum(
        (request_total * rescale, request_accum * rescale[..., None]), "tensor"
    )
    context = finish_context(maxima, totals, accum, query_all, entries_all)
    projected = jnp.dot(context, out_proj, preferred_element_type=jnp.float32)
    column_block = projected.shape[1]
    arrived = lax.all_to_all(
        projected.reshape(tensor_count, dec_rows, column_block),
        "tensor",
        split_axis=0,
        concat_axis=2,
        tiled=True,
    )
    widened = stream.astype(jnp.float32)
    widened = widened.at[:dec_rows].add(arrived[0])
    resid = lax.optimization_barrier(widened.astype(jnp.bfloat16))
    widened = resid.astype(jnp.float32)
    inverse = lax.rsqrt(jnp.mean(widened * widened, axis=-1, keepdims=True) + EPSILON)
    normed = (widened * inverse * norm_gain.astype(jnp.float32)).astype(jnp.bfloat16)
    logits = jnp.dot(normed, router, preferred_element_type=jnp.float32)
    chosen = jnp.take_along_axis(logits, routes, axis=1)
    gate_probs = jax.nn.softmax(chosen, axis=-1)
    expert_count = tensor_count // GROUP
    expert_ids = jnp.arange(expert_count, dtype=jnp.int32)
    matched = routes[:, :, None] == expert_ids[None, None, :]
    routed = jnp.any(matched, axis=1)
    gate_weight = jnp.sum(jnp.where(matched, gate_probs[:, :, None], 0.0), axis=1)
    routed_count = routed.astype(jnp.int32)
    ranking = jnp.cumsum(routed_count, axis=0) - routed_count
    slot_ids = jnp.arange(CAP, dtype=jnp.int32)
    selector = routed.T[:, None, :] & (ranking.T[:, None, :] == slot_ids[None, :, None])
    slot_rows = jnp.einsum(
        "eci,id->ecd", selector.astype(jnp.bfloat16), normed, preferred_element_type=jnp.float32
    ).astype(jnp.bfloat16)
    outgoing = jnp.repeat(slot_rows, GROUP, axis=0)
    contract_last = (((1,), (1,)), ((), ()))
    incoming = lax.all_to_all(outgoing, "tensor", split_axis=0, concat_axis=0, tiled=True)
    shape_in = incoming.shape
    flat_rows = incoming.reshape(-1, shape_in[2])
    gate_part = lax.dot_general(
        flat_rows, gate_up[0], contract_last, preferred_element_type=jnp.float32
    )
    upward = lax.dot_general(
        flat_rows, gate_up[1], contract_last, preferred_element_type=jnp.float32
    )
    active = (jax.nn.silu(gate_part) * upward).astype(jnp.bfloat16)
    partial_value = jnp.dot(active, down_proj, preferred_element_type=jnp.float32).astype(
        jnp.bfloat16
    )
    returned = lax.all_to_all(
        partial_value.reshape(shape_in), "tensor", split_axis=0, concat_axis=0, tiled=True
    )
    expert_out = jnp.sum(
        returned.reshape(expert_count, GROUP, CAP, returned.shape[2]), axis=1, dtype=jnp.float32
    )
    weighted = selector.astype(jnp.float32) * gate_weight.T[:, None, :]
    routed_sum = jnp.einsum("eci,ecd->id", weighted, expert_out)
    return (widened + routed_sum).astype(jnp.bfloat16)


def solution(mesh):
    placed = (
        P(("dp", "tensor"), None),
        P(("dp", "tensor"), None),
        P(("dp", "tensor"), None),
        P(("dp", "tensor"), None, None, None),
        P("dp", None),
        P("dp"),
        P(None, "tensor"),
        P(),
        P(),
        P(("dp", "tensor"), None),
        P(None, "tensor", None),
        P("tensor", None),
    )
    return jax.shard_map(
        local, mesh=mesh, in_specs=placed, out_specs=P(("dp", "tensor"), None), check_vma=False
    )
```

profile of v0, /device:TPU:40, one launch (start us, length us, event | category | flops | bytes accessed | tf_op | source)
XLA Modules:
  0.0 1744.6 jit_solution(13407701293075123612)
XLA Ops:
  6.5 1.1 fusion.28
  8.4 106.0 %all-gather = bf16[128,1,2560]{2,1,0:T(2,128)(2,1)S(1)} all-gather(bf16[1,1,2560]{2,1,0:T(2,128)(2,1)} %bitcast.71), channel_id=1, replica_groups=mesh['dp'=4,'tensor'=128] {'tensor'}, dimensions={0}, use_global_device_ids=true | all-gather | bytes 660480 | tf_op jit(solution)/shard_map/all_gather | solution.py:105
  115.5 2.3 fusion.59
  117.8 2.2 copy.144
  119.9 1.1 copy.143
  121.1 1.4 fusion.60
  122.9 1.6 fusion.31
  124.7 419.6 %pmax.7 = f32[128,4,5]{0,2,1:T(8,128)S(1)} all-reduce(f32[128,4,5]{0,2,1:T(8,128)S(1)} %select_reduce_fusion), channel_id=1, replica_groups=mesh['dp'=4,'tensor'=128] {'tensor'}, use_global_device_ids=true, to_apply=%region_5.6 | all-reduce | flops 2560 | bytes 20480 | tf_op jit(solution)/shard_map/pmax | solution.py:111
  544.4 1.5 fusion.2
  546.0 153.4 %all-gather.1 = bf16[128,1,1024]{2,1,0:T(2,128)(2,1)S(1)} all-gather(bf16[1,1,1024]{2,1,0:T(2,128)(2,1)S(1)} %bitcast.72), channel_id=1, replica_groups=mesh['dp'=4,'tensor'=128] {'tensor'}, dimensions={0}, use_global_device_ids=true | all-gather | bytes 264192 | tf_op jit(solution)/shard_map/all_gather | solution.py:106
  701.1 420.0 %psum.15 = f32[128,4,5]{0,2,1:T(8,128)S(1)} all-reduce(f32[128,4,5]{0,2,1:T(8,128)S(1)} %get-tuple-element.20), channel_id=1, replica_groups=mesh['dp'=4,'tensor'=128] {'tensor'}, use_global_device_ids=true, to_apply=%region_9.10 | all-reduce | flops 2560 | bytes 20480 | tf_op jit(solution)/shard_map/psum | solution.py:113
  1121.3 1.6 divide_convert_fusion
  1123.9 81.8 %all-to-all-start = ((f32[128,1,20]{2,1,0:T(1,128)}), f32[128,1,20]{2,1,0:T(1,128)S(1)}, u32[]{:S(2)}, u32[]{:S(2)}) async-start(f32[128,1,20]{2,1,0:T(1,128)} %bitcast.25), calls=%async_computation | async-start | bytes 131072 | tf_op jit(solution)/shard_map/all_to_all | solution.py:119
  1205.8 13.6 all-to-all-done
  1222.3 243.3 %all_to_all.19 = bf16[128,6,2560]{2,1,0:T(8,128)(2,1)} all-to-all(bf16[128,6,2560]{2,1,0:T(8,128)(2,1)S(1)} %bitcast.61), channel_id=1, replica_groups=mesh['dp'=4,'tensor'=128] {'tensor'}, dimensions={0} | all-to-all | bytes 7864320 | tf_op jit(solution)/shard_map/all_to_all | solution.py:149
  1465.7 7.3 reshape.163
  1472.9 3.8 fusion.7
  1476.7 7.5 convolution_convert_fusion
  1484.2 7.1 reshape.164
  1491.3 7.9 all-to-all-start.2
  1499.8 2.9 gather_fusion
  1503.0 230.2 %all-to-all-done.2 = bf16[128,6,2560]{2,1,0:T(8,128)(2,1)} async-done(((bf16[128,6,2560]{2,1,0:T(8,128)(2,1)}), bf16[128,6,2560]{2,1,0:T(8,128)(2,1)}, u32[]{:S(2)}, u32[]{:S(2)}) %all-to-all-start.2) | async-done | bytes 3932192 | tf_op jit(solution)/shard_map/all_to_all | solution.py:162
  1733.2 3.5 convert_reduce_fusion
  1736.7 1.0 fusion.1
  (68 shorter events, 9.3 us)
Async XLA Ops:
  6.5 1470.2 %copy-start = (bf16[192,2560]{1,0:T(8,128)(2,1)S(1)}, bf16[192,2560]{1,0:T(8,128)(2,1)}, u32[]{:S(2)}) copy-start(bf16[192,2560]{1,0:T(8,128)(2,1)} %param.25) | copy-start | bytes 2949124
  6.5 1114.7 %all-reduce.2.cloned.1.call-start = ((), (), s32[]{:S(2)}) async-start(), calls=%async_computation.3 | async-start | bytes 2621440 | tf_op jit(solution)/shard_map/psum | solution.py:113
  122.5 423.5 %copy-start.2 = (s32[64,6]{0,1:T(8,128)S(1)}, s32[64,6]{0,1:T(8,128)}, u32[]{:S(2)}) copy-start(s32[64,6]{0,1:T(8,128)} %param.23) | copy-start | bytes 4612
  122.5 423.5 %copy-start.5 = (bf16[1,1024]{1,0:T(2,128)(2,1)S(1)}, bf16[1,1024]{1,0:T(2,128)(2,1)}, u32[]{:S(2)}) copy-start(bf16[1,1024]{1,0:T(2,128)(2,1)} %param.16) | copy-start | bytes 6148
  700.9 421.9 %copy-start.3 = (bf16[2560,20]{0,1:T(8,128)(2,1)S(1)}, bf16[2560,20]{0,1:T(8,128)(2,1)}, u32[]{:S(2)}) copy-start(bf16[2560,20]{0,1:T(8,128)(2,1)} %param.20) | copy-start | bytes 307204
  1121.1 84.6 %copy-start.4 = (bf16[2560]{0:T(1024)(128)(2,1)S(1)}, bf16[2560]{0:T(1024)(128)(2,1)}, u32[]{:S(2)}) copy-start(bf16[2560]{0:T(1024)(128)(2,1)} %param.21) | copy-start | bytes 15364
  1121.1 84.6 %copy-start.1 = (bf16[64,2560]{1,0:T(8,128)(2,1)S(1)}, bf16[64,2560]{1,0:T(8,128)(2,1)}, u32[]{:S(2)}) copy-start(bf16[64,2560]{1,0:T(8,128)(2,1)} %param.14) | copy-start | bytes 983044
  1123.9 95.5 %all-to-all-start = ((f32[128,1,20]{2,1,0:T(1,128)}), f32[128,1,20]{2,1,0:T(1,128)S(1)}, u32[]{:S(2)}, u32[]{:S(2)}) async-start(f32[128,1,20]{2,1,0:T(1,128)} %bitcast.25), calls=%async_computation | async-start | bytes 131072 | tf_op jit(solution)/shard_map/all_to_all | solution.py:119
  1491.3 8.2 copy-start.6
  1491.3 241.9 %all-to-all-start.2 = ((bf16[128,6,2560]{2,1,0:T(8,128)(2,1)}), bf16[128,6,2560]{2,1,0:T(8,128)(2,1)}, u32[]{:S(2)}, u32[]{:S(2)}) async-start(bf16[128,6,2560]{2,1,0:T(8,128)(2,1)} %reshape.164), calls=%async_computation.2 | async-start | bytes 10485760 | tf_op jit(solution)/shard_map/all_to_all | solution.py:162
Sparse Core Ops, SparseCore 0:
  546.1 408.8 all-reduce.1
where the time goes:
time: 1750 us; the launch traced here: 1740 us
  blocking collectives  1340 us (77%)
  waiting for transfers between devices  244 us (14%)
  starting transfers between devices  89.7 us (5%)
  local copies, waits for them, and re-layouts  26.5 us (2%)
  matrix products  18.7 us (1%)
    psum x1, blocking collectives, local(): lax.psum((request_total * rescale, request_accum * rescale[..., None]), '...  420 us
    pmax x1, blocking collectives, local(): maxima = lax.pmax(request_max, 'tensor')  420 us
    all_to_all x1, blocking collectives, local(): lax.all_to_all(outgoing, 'tensor', split_axis=0, concat_axis=0, tiled=True)  243 us
    all_to_all x1, waiting for transfers between devices, local(): lax.all_to_all(partial_value.reshape(shape_in), 'tensor', split_axis=0, c...  230 us
    all_gather x1, blocking collectives, local(): lax.all_gather(fresh_entries, 'tensor', axis=0, tiled=True)  153 us
    all_gather x1, blocking collectives, local(): lax.all_gather(queries, 'tensor', axis=0, tiled=True)  106 us
    all_to_all x1, starting transfers between devices, local(): lax.all_to_all(projected.reshape(tensor_count, dec_rows, column_block), '...  81.8 us
  transfers between devices with their start and end apart: 3, of which 2 were waited for; matrix products, arithmetic and copies ran while one was open for 0% of the time, Pallas kernels for 0%

commit v1 on v0

--- a/solution.py
+++ b/solution.py
@@ -11,6 +11,13 @@
 CAP = 6
 NEG_FILL = -1e30
 EPSILON = 1e-05
+
+
+def all_by_exchange(array, name, along):
+    devices = lax.axis_size(name)
+    blocks = jnp.stack([array for _ in range(devices)])
+    blocks = lax.all_to_all(blocks, name, split_axis=0, concat_axis=0)
+    return jnp.concatenate(blocks, axis=along)
 
 
 def finish_context(maxima, totals, accum, local_queries, local_entries):
@@ -103,7 +110,7 @@
     dec_rows = queries.shape[0]
     query_all, entries_all = (
         lax.all_gather(queries, "tensor", axis=0, tiled=True),
-        lax.all_gather(fresh_entries, "tensor", axis=0, tiled=True),
+        all_by_exchange(fresh_entries, "tensor", 0),
     )
     request_max, request_total, request_accum = local_parts(
         query_all, paged_store_cache, page_table, cache_length, my_index

time: 1750 us -> 1690 us (0.966)
  blocking collectives: 1340 us -> 1260 us
  starting transfers between devices: 89.7 us -> 109 us
    all_gather x1 -> x0, blocking collectives: 153 us -> none  [local(): lax.all_gather(fresh_entries, 'tensor', axis=0, tiled=True)]
    psum x1, blocking collectives: 420 us -> 491 us  [local(): lax.psum((request_total * rescale, request_accum * rescale[..., None]), '...]
    all_to_all x0 -> x1, starting transfers between devices: none -> 19.2 us  [all_by_exchange(): blocks = lax.all_to_all(blocks, name, split_axis=0, concat_axis=0)]
  transfers between devices with their start and end apart: 3 -> 4, of which waited for: 2 -> 2; matrix products, arithmetic and copies ran while one was open for 0% -> 1% of each run, Pallas kernels for 0% -> 0%
where the time goes in v1:
time: 1690 us; the launch traced here: 1680 us
  blocking collectives  1260 us (75%)
  waiting for transfers between devices  244 us (14%)
  starting transfers between devices  109 us (6%)
  local copies, waits for them, and re-layouts  28.4 us (2%)
  matrix products  18.7 us (1%)
    psum x1, blocking collectives, local(): lax.psum((request_total * rescale, request_accum * rescale[..., None]), '...  491 us
    pmax x1, blocking collectives, local(): maxima = lax.pmax(request_max, 'tensor')  418 us
    all_to_all x1, blocking collectives, local(): lax.all_to_all(outgoing, 'tensor', split_axis=0, concat_axis=0, tiled=True)  243 us
    all_to_all x1, waiting for transfers between devices, local(): lax.all_to_all(partial_value.reshape(shape_in), 'tensor', split_axis=0, c...  230 us
    all_gather x1, blocking collectives, local(): lax.all_gather(queries, 'tensor', axis=0, tiled=True)  108 us
    all_to_all x1, starting transfers between devices, local(): lax.all_to_all(projected.reshape(tensor_count, dec_rows, column_block), '...  81.6 us
  transfers between devices with their start and end apart: 4, of which 2 were waited for; matrix products, arithmetic and copies ran while one was open for 1% of the time, Pallas kernels for 0%

profile of v1, /device:TPU:40, one launch (start us, length us, event | category | flops | bytes accessed | tf_op | source)
XLA Modules:
  0.0 1684.7 jit_solution(8332447780211166732)
XLA Ops:
  8.1 2.1 reduce.9
  11.2 19.2 %all-to-all-start = ((bf16[128,2,512]{2,1,0:T(2,128)(2,1)}), bf16[128,2,512]{2,1,0:T(2,128)(2,1)S(1)}, u32[]{:S(2)}, u32[]{:S(2)}) async-start(bf16[128,2,512]{2,1,0:T(2,128)(2,1)} %reshape.202), calls=%async_computation | async-start | bytes 524288 | tf_op jit(solution)/shard_map/all_to_all | solution.py:19
  30.8 107.7 %all-gather = bf16[128,1,2560]{2,1,0:T(2,128)(2,1)S(1)} all-gather(bf16[1,1,2560]{2,1,0:T(2,128)(2,1)S(1)} %bitcast.70), channel_id=1, replica_groups=mesh['dp'=4,'tensor'=128] {'tensor'}, dimensions={0}, use_global_device_ids=true | all-gather | bytes 660480 | tf_op jit(solution)/shard_map/all_gather | solution.py:112
  138.9 2.3 fusion.59
  141.1 2.2 copy.126
  143.3 1.1 copy.125
  144.5 1.4 fusion.60
  146.5 418.4 %pmax.7 = f32[128,4,5]{0,2,1:T(8,128)S(1)} all-reduce(f32[128,4,5]{0,2,1:T(8,128)S(1)} %select_reduce_fusion), channel_id=1, replica_groups=mesh['dp'=4,'tensor'=128] {'tensor'}, use_global_device_ids=true, to_apply=%region_5.6 | all-reduce | flops 2560 | bytes 20480 | tf_op jit(solution)/shard_map/pmax | solution.py:118
  565.0 1.6 fusion.31
  566.6 1.6 fusion.2
  569.4 491.2 %psum.15 = f32[128,4,5]{0,2,1:T(8,128)S(1)} all-reduce(f32[128,4,5]{0,2,1:T(8,128)S(1)} %get-tuple-element.20), channel_id=1, replica_groups=mesh['dp'=4,'tensor'=128] {'tensor'}, use_global_device_ids=true, to_apply=%region_9.10 | all-reduce | flops 2560 | bytes 20480 | tf_op jit(solution)/shard_map/psum | solution.py:120
  1061.6 1.6 divide_convert_fusion
  1064.2 81.6 %all-to-all-start.1 = ((f32[128,1,20]{2,1,0:T(1,128)}), f32[128,1,20]{2,1,0:T(1,128)S(1)}, u32[]{:S(2)}, u32[]{:S(2)}) async-start(f32[128,1,20]{2,1,0:T(1,128)} %bitcast.24), calls=%async_computation.1 | async-start | bytes 131072 | tf_op jit(solution)/shard_map/all_to_all | solution.py:126
  1145.9 13.6 all-to-all-done.1
  1162.4 243.3 %all_to_all.24 = bf16[128,6,2560]{2,1,0:T(8,128)(2,1)} all-to-all(bf16[128,6,2560]{2,1,0:T(8,128)(2,1)S(1)} %bitcast.60), channel_id=1, replica_groups=mesh['dp'=4,'tensor'=128] {'tensor'}, dimensions={0} | all-to-all | bytes 7864320 | tf_op jit(solution)/shard_map/all_to_all | solution.py:156
  1405.8 7.3 reshape.170
  1413.0 3.8 fusion.7
  1416.8 7.5 convolution_convert_fusion
  1424.3 7.1 reshape.171
  1431.4 7.9 all-to-all-start.3
  1439.9 2.9 gather_fusion
  1443.1 230.2 %all-to-all-done.3 = bf16[128,6,2560]{2,1,0:T(8,128)(2,1)} async-done(((bf16[128,6,2560]{2,1,0:T(8,128)(2,1)}), bf16[128,6,2560]{2,1,0:T(8,128)(2,1)}, u32[]{:S(2)}, u32[]{:S(2)}) %all-to-all-start.3) | async-done | bytes 3932192 | tf_op jit(solution)/shard_map/all_to_all | solution.py:169
  1673.3 3.5 convert_reduce_fusion
  1676.8 1.0 fusion.1
  (79 shorter events, 10.9 us)
Async XLA Ops:
  6.5 1410.3 %copy-start = (bf16[192,2560]{1,0:T(8,128)(2,1)S(1)}, bf16[192,2560]{1,0:T(8,128)(2,1)}, u32[]{:S(2)}) copy-start(bf16[192,2560]{1,0:T(8,128)(2,1)} %param.25) | copy-start | bytes 2949124
  6.5 23.9 %copy-start.4 = (s32[128,32]{0,1:T(8,128)S(1)}, s32[128,32]{0,1:T(8,128)}, u32[]{:S(2)}) copy-start(s32[128,32]{0,1:T(8,128)} %param.18) | copy-start | bytes 49156
  6.5 24.3 %copy-start.5 = (bf16[1,2560]{1,0:T(2,128)(2,1)S(1)}, bf16[1,2560]{1,0:T(2,128)(2,1)}, u32[]{:S(2)}) copy-start(bf16[1,2560]{1,0:T(2,128)(2,1)} %param.15) | copy-start | bytes 15364
  6.5 132.0 %copy-start.7 = (s32[128]{0:T(128)S(1)}, s32[128]{0:T(128)}, u32[]{:S(2)}) copy-start(s32[128]{0:T(128)} %param.19) | copy-start | bytes 1540
  11.2 1049.5 %all-to-all-start = ((bf16[128,2,512]{2,1,0:T(2,128)(2,1)}), bf16[128,2,512]{2,1,0:T(2,128)(2,1)S(1)}, u32[]{:S(2)}, u32[]{:S(2)}) async-start(bf16[128,2,512]{2,1,0:T(2,128)(2,1)} %reshape.202), calls=%async_computation | async-start | bytes 524288 | tf_op jit(solution)/shard_map/all_to_all | solution.py:19
  30.3 1031.2 %all-reduce.2.cloned.1.call-start = ((), (), s32[]{:S(2)}) async-start(), calls=%async_computation.4 | async-start | bytes 2621440 | tf_op jit(solution)/shard_map/psum | solution.py:120
  145.9 422.3 %copy-start.2 = (s32[64,6]{0,1:T(8,128)S(1)}, s32[64,6]{0,1:T(8,128)}, u32[]{:S(2)}) copy-start(s32[64,6]{0,1:T(8,128)} %param.23) | copy-start | bytes 4612
  1061.1 2.0 copy-start.3
  1061.3 84.5 %copy-start.6 = (bf16[2560]{0:T(1024)(128)(2,1)S(1)}, bf16[2560]{0:T(1024)(128)(2,1)}, u32[]{:S(2)}) copy-start(bf16[2560]{0:T(1024)(128)(2,1)} %param.21) | copy-start | bytes 15364
  1061.3 84.5 %copy-start.1 = (bf16[64,2560]{1,0:T(8,128)(2,1)S(1)}, bf16[64,2560]{1,0:T(8,128)(2,1)}, u32[]{:S(2)}) copy-start(bf16[64,2560]{1,0:T(8,128)(2,1)} %param.14) | copy-start | bytes 983044
  1064.2 95.3 %all-to-all-start.1 = ((f32[128,1,20]{2,1,0:T(1,128)}), f32[128,1,20]{2,1,0:T(1,128)S(1)}, u32[]{:S(2)}, u32[]{:S(2)}) async-start(f32[128,1,20]{2,1,0:T(1,128)} %bitcast.24), calls=%async_computation.1 | async-start | bytes 131072 | tf_op jit(solution)/shard_map/all_to_all | solution.py:126
  1431.4 8.2 copy-start.8
  1431.4 241.9 %all-to-all-start.3 = ((bf16[128,6,2560]{2,1,0:T(8,128)(2,1)}), bf16[128,6,2560]{2,1,0:T(8,128)(2,1)}, u32[]{:S(2)}, u32[]{:S(2)}) async-start(bf16[128,6,2560]{2,1,0:T(8,128)(2,1)} %reshape.171), calls=%async_computation.3 | async-start | bytes 10485760 | tf_op jit(solution)/shard_map/all_to_all | solution.py:169
Sparse Core Ops, SparseCore 0:
  568.3 407.9 all-reduce.1
